TPU v7x, 512 devices: a whole 4x8x8 slice. The times are simulated.
512 devices in a mesh: dp: 16 (over z_hi, y), tensor: 32 (over x, z_lo, core).
Axes of the slice: x: 4, y: 8, z: 8 (z_hi: 2, z_lo: 4; z = z_hi * 4 + z_lo), core: 2. Of those that a mesh axis runs over, the one named last changes fastest.
Arguments:
- suffix_states: bfloat16 [32, 128, 2048], P(None, 'dp', 'tensor'), may hold values from -16 to 16
- suffix_lengths: int32 [32], replicated, may hold values from 1 to 128, 2560 in all
- request_group: int32 [32, 1], replicated, may hold values from 0 to 15
- group_owner: int32 [16], replicated, may hold values from 0 to 15, each once
- request_order: int32 [32], replicated, may hold values from 0 to 31, each once
- prefix_cache: bfloat16 [16, 256, 1024], P('dp', 'tensor'), may hold values from -700 to 700
- norm_attn: bfloat16 [2048], replicated, may hold values from 0.099609375 to 1.8984375
- w_query: bfloat16 [2048, 2048], P(None, 'tensor'), may hold values from -0.125 to 0.125
- w_key: bfloat16 [2048, 512], P(None, 'tensor'), may hold values from -0.125 to 0.125
- w_value: bfloat16 [2048, 512], P(None, 'tensor'), may hold values from -0.125 to 0.125
- w_out: bfloat16 [2048, 2048], P('tensor'), may hold values from -0.25 to 0.25
- norm_mlp: bfloat16 [2048], replicated, may hold values from 0.099609375 to 1.8984375
- w_gate: bfloat16 [2048, 8192], P(None, 'tensor'), may hold values from -0.125 to 0.125
- w_up: bfloat16 [2048, 8192], P(None, 'tensor'), may hold values from -0.125 to 0.125
- w_down: bfloat16 [8192, 2048], P('tensor'), may hold values from -0.125 to 0.125
Outputs:
- hidden_out: bfloat16 [32, 128, 2048], P(None, 'dp', 'tensor')
- suffix_keys: bfloat16 [32, 128, 512], P('dp', None, 'tensor')
- suffix_values: bfloat16 [32, 128, 512], P('dp', None, 'tensor')
Inputs may be any that keep to these rules, and one draw needn't show every extreme that they name: `suffix_lengths`: the lengths sum to 2560 and some request has exactly 128. `request_group`: every group has at least one request. `group_owner`: A permutation of the 16 groups onto the slots of prefix_cache. `request_order`: A permutation of the requests; slot s belongs to index s // 2 of dp.
All inputs are finite; a program needn't handle non-finite values.
Results may differ from a plain program's by a relative error of at most 0.03.
Values may be sent and summed in bfloat16 or wider, within the bound.
No kernel may reach another device: no remote copies, remote signals or barrier semaphores. Data moves between devices by JAX's collectives and lax.ppermute only.
A program may use at most 64 MiB of HBM per device.

v0:
```python
import jax
import jax.numpy as jnp
import numpy as np
from jax import lax
from jax.sharding import PartitionSpec as P

H = 32
KVH = 8
HD = 64
L_MAX = 128
P_SIZE = 256
THETA = 10000000.0
EPSILON = 1e-05


def rms_scale(states, gain):
    wide = states.astype(jnp.float32)
    mean_square = jnp.mean(wide * wide, axis=-1, keepdims=True)
    return (wide * lax.rsqrt(mean_square + EPSILON) * gain.astype(jnp.float32)).astype(jnp.bfloat16)


def rotate(vectors, positions):
    half = HD // 2
    freqs = THETA ** (-(jnp.arange(half, dtype=jnp.float32) * 2.0 / HD))
    angles = positions[:, None] * freqs[None, :]
    cosine = jnp.cos(angles)[:, None, :]
    sine = jnp.sin(angles)[:, None, :]
    first = vectors[..., :half]
    second = vectors[..., half:]
    return jnp.concatenate(
        [first * cosine - second * sine, second * cosine + first * sine], axis=-1
    )


def absorb_block(state_now, scores, allowed, value_rows):
    running_max, running_sum, numerator = state_now
    block_max = jnp.max(jnp.where(allowed, scores, -1e30), axis=2)
    new_max = jnp.maximum(running_max, block_max)
    rescale = jnp.exp(running_max - new_max)
    weights = jnp.where(allowed, jnp.exp(scores - new_max[:, :, None]), 0.0)
    running_sum = running_sum * rescale + jnp.sum(weights, axis=2)
    numerator = numerator * rescale[:, :, None] + jnp.einsum(
        "htk,khd->htd", weights.astype(jnp.bfloat16), value_rows, preferred_element_type=jnp.float32
    )
    return (new_max, running_sum, numerator)


def shards(
    suffix_states,
    suffix_lengths,
    request_group,
    group_owner,
    request_order,
    prefix_cache,
    norm_attn,
    w_query,
    w_key,
    w_value,
    w_out,
    norm_mlp,
    w_gate,
    w_up,
    w_down,
):
    dp_count = lax.axis_size("dp")
    tp_count = lax.axis_size("tensor")
    dp_index = lax.axis_index("dp")
    tp_index = lax.axis_index("tensor")
    total_reqs = suffix_lengths.shape[0]
    local_reqs = total_reqs // dp_count
    row_count = local_reqs * L_MAX
    heads_here = w_query.shape[1] // HD
    group_size = H // KVH
    kv_here = max(1, heads_here // group_size)
    slab_width = kv_here * 2 * HD
    score_scale = HD ** (-0.5)
    head_map = np.arange(heads_here) // group_size
    dest_table = (
        np.arange(tp_count)[:, None] * heads_here // group_size + np.arange(kv_here)[None, :]
    ).reshape(-1)
    routed = jnp.take(suffix_states, request_order, axis=0)
    routed_here = lax.all_to_all(routed, "dp", split_axis=0, concat_axis=1, tiled=True)
    width_here = routed_here.shape[2]
    state_shard = routed_here.reshape(row_count, width_here)
    slot_ids = dp_index * local_reqs + jnp.arange(local_reqs, dtype=jnp.int32)
    req_ids = jnp.take(request_order, slot_ids)
    lengths_here = jnp.take(suffix_lengths, req_ids)
    owner_here = jnp.take(group_owner, jnp.take(request_group[:, 0], req_ids))
    position = jnp.arange(L_MAX, dtype=jnp.int32)
    valid = (position[None, :] < lengths_here[:, None]).reshape(row_count)
    positions = (P_SIZE + jnp.tile(position, local_reqs)).astype(jnp.float32)
    full_rows = lax.all_gather(state_shard, "tensor", axis=1, tiled=True)
    normed = rms_scale(full_rows, norm_attn)
    query = rotate(
        jnp.dot(normed, w_query, preferred_element_type=jnp.float32).reshape(
            row_count, heads_here, HD
        ),
        positions,
    ).astype(jnp.bfloat16)
    key_part = jnp.dot(normed, w_key, preferred_element_type=jnp.float32).astype(jnp.bfloat16)
    value_part = jnp.dot(normed, w_value, preferred_element_type=jnp.float32).astype(jnp.bfloat16)
    key_full, value_full = (
        lax.all_gather(key_part, "tensor", axis=1, tiled=True),
        lax.all_gather(value_part, "tensor", axis=1, tiled=True),
    )
    key_heads = key_full.reshape(row_count, HD, KVH).transpose(0, 2, 1)
    value_heads = value_full.reshape(row_count, HD, KVH).transpose(0, 2, 1)
    key_rot = rotate(key_heads.astype(jnp.float32), positions).astype(jnp.bfloat16)
    cache_width = key_part.shape[1]
    keys_flat = jnp.where(valid[:, None], key_rot.reshape(row_count, KVH * HD), 0.0)
    values_flat = jnp.where(valid[:, None], value_heads.reshape(row_count, KVH * HD), 0.0)
    keys_out = lax.dynamic_slice_in_dim(keys_flat, tp_index * cache_width, cache_width, 1).reshape(
        local_reqs, L_MAX, cache_width
    )
    values_out = lax.dynamic_slice_in_dim(
        values_flat, tp_index * cache_width, cache_width, 1
    ).reshape(local_reqs, L_MAX, cache_width)
    kv_first = tp_index * heads_here // group_size
    own_keys = lax.dynamic_slice_in_dim(key_rot, kv_first, kv_here, 1)[:, head_map].reshape(
        local_reqs, L_MAX, heads_here, HD
    )
    own_values = lax.dynamic_slice_in_dim(value_heads, kv_first, kv_here, 1)[:, head_map].reshape(
        local_reqs, L_MAX, heads_here, HD
    )
    query_req = query.reshape(local_reqs, L_MAX, heads_here, HD)

    def absorb_prefix(state_one, query_one, slot_block):
        block = slot_block.reshape(slot_block.shape[0], kv_here, 2, HD)
        key_rows = block[:, head_map, 0]
        value_rows = block[:, head_map, 1]
        scores = (
            jnp.einsum("thd,phd->htp", query_one, key_rows, preferred_element_type=jnp.float32)
            * score_scale
        )
        return absorb_block(state_one, scores, jnp.ones((1, 1, 1), bool), value_rows)

    initial = tuple(
        (
            (
                jnp.full((heads_here, L_MAX), -1e30, jnp.float32),
                jnp.zeros((heads_here, L_MAX), jnp.float32),
                jnp.zeros((heads_here, L_MAX, HD), jnp.float32),
            )
            for request in range(local_reqs)
        )
    )
    all_rows = lax.all_gather(prefix_cache, "dp", axis=0, tiled=True)
    rows_each = all_rows.shape[1]
    chosen = jnp.take(all_rows.reshape(dp_count, rows_each, KVH, 2 * HD), dest_table, axis=2)
    picked = lax.all_to_all(chosen, "tensor", split_axis=2, concat_axis=1, tiled=True).reshape(
        dp_count, P_SIZE, slab_width
    )
    states = tuple(
        (
            absorb_prefix(
                initial[request],
                query_req[request],
                lax.dynamic_index_in_dim(picked, owner_here[request], 0, keepdims=False),
            )
            for request in range(local_reqs)
        )
    )
    pieces = []
    for request in range(local_reqs):
        self_scores = (
            jnp.einsum(
                "thd,shd->hts",
                query_req[request],
                own_keys[request],
                preferred_element_type=jnp.float32,
            )
            * score_scale
        )
        self_allowed = (position[None, :] <= position[:, None]) & (
            position[None, :] < lengths_here[request]
        )
        running_max, running_sum, numerator = absorb_block(
            states[request], self_scores, self_allowed[None], own_values[request]
        )
        attention_one = (numerator / running_sum[:, :, None]).astype(jnp.bfloat16)
        pieces.append(attention_one.transpose(1, 0, 2).reshape(L_MAX, heads_here * HD))
    attention = jnp.concatenate(pieces, axis=0)
    attn_terms = jnp.dot(attention, w_out, preferred_element_type=jnp.float32)
    attn_share = lax.psum_scatter(
        attn_terms.astype(jnp.bfloat16), "tensor", scatter_dimension=1, tiled=True
    ).astype(jnp.float32)
    middle = (state_shard.astype(jnp.float32) + attn_share).astype(jnp.bfloat16)
    middle_rows = lax.all_gather(middle, "tensor", axis=1, tiled=True)
    normed_two = rms_scale(middle_rows, norm_mlp)
    gate = jnp.dot(normed_two, w_gate, preferred_element_type=jnp.float32)
    upper = jnp.dot(normed_two, w_up, preferred_element_type=jnp.float32)
    hidden = (jax.nn.silu(gate) * upper).astype(jnp.bfloat16)
    down_terms = jnp.dot(hidden, w_down, preferred_element_type=jnp.float32)
    down_share = lax.psum_scatter(
        down_terms.astype(jnp.bfloat16), "tensor", scatter_dimension=1, tiled=True
    ).astype(jnp.float32)
    result = middle.astype(jnp.float32) + down_share
    result = (
        jnp.where(valid[:, None], result, 0.0)
        .astype(jnp.bfloat16)
        .reshape(local_reqs, L_MAX, width_here)
    )
    returned = lax.all_to_all(result, "dp", split_axis=1, concat_axis=0, tiled=True)
    hidden_out = jnp.zeros_like(returned).at[request_order].set(returned)
    return (hidden_out, keys_out, values_out)


def solution(mesh):
    in_specs = (
        P(None, "dp", "tensor"),
        P(),
        P(),
        P(),
        P(),
        P("dp", "tensor", None),
        P(),
        P(None, "tensor"),
        P(None, "tensor"),
        P(None, "tensor"),
        P("tensor", None),
        P(),
        P(None, "tensor"),
        P(None, "tensor"),
        P("tensor", None),
    )
    out_specs = (P(None, "dp", "tensor"), P("dp", None, "tensor"), P("dp", None, "tensor"))
    return jax.shard_map(shards, mesh=mesh, in_specs=in_specs, out_specs=out_specs, check_vma=False)
```

profile of v0, /device:TPU:8, one launch (start us, length us, event | category | flops | bytes accessed | tf_op | source)
XLA Modules:
  0.0 635.4 jit_solution(12212164289237570744)
XLA Ops:
  7.2 0.7 compare_select_fusion.3
  7.9 0.7 compare_and_fusion.1
  8.6 1.4 gather_fusion
  10.1 0.7 reshape.707
  10.9 16.0 %all-to-all-start = ((bf16[16,2,512]{2,1,0:T(2,128)(2,1)}), bf16[16,2,512]{2,1,0:T(2,128)(2,1)S(1)}, u32[]{:S(2)}, u32[]{:S(2)}) async-start(bf16[16,2,512]{2,1,0:T(2,128)(2,1)} %reshape.707), calls=%async_computation | async-start | bytes 65536 | tf_op jit(solution)/shard_map/all_to_all | solution.py:82
  26.9 49.1 %all_gather.16 = bf16[16,8,1024]{2,1,0:T(8,128)(2,1)S(1)} all-gather(bf16[1,8,1024]{2,1,0:T(8,128)(2,1)} %param.30), channel_id=1, replica_groups=mesh['dp'=16,'tensor'=32] {'dp'}, dimensions={0}, use_global_device_ids=true | all-gather | bytes 278528 | tf_op jit(solution)/shard_map/all_gather | solution.py:147
  76.0 0.7 pad_clamp_fusion.1
  76.7 1.9 gather_fusion.1
  78.6 6.7 %all-to-all-start.1 = ((bf16[16,8,32,128]{3,1,0,2:T(8,128)(2,1)}), bf16[16,8,32,128]{3,1,0,2:T(8,128)(2,1)S(1)}, u32[]{:S(2)}, u32[]{:S(2)}) async-start(bf16[16,8,32,128]{3,1,0,2:T(8,128)(2,1)} %bitcast.9), calls=%async_computation.1 | async-start | bytes 2097152 | tf_op jit(solution)/shard_map/all_to_all | solution.py:150
  85.4 0.6 gather_fusion.3
  86.1 0.7 copy.51
  87.0 0.6 gather_fusion.5
  87.6 0.6 gather_fusion.4
  88.3 0.6 gather_fusion.2
  88.9 0.6 fusion.81
  93.5 0.6 fusion.80
  94.1 0.6 iota_compare_fusion.2
  94.7 0.7 iota_compare_fusion.1
  95.6 17.5 %all-to-all-done.1 = bf16[16,8,32,128]{3,1,0,2:T(8,128)(2,1)S(1)} async-done(((bf16[16,8,32,128]{3,1,0,2:T(8,128)(2,1)}), bf16[16,8,32,128]{3,1,0,2:T(8,128)(2,1)S(1)}, u32[]{:S(2)}, u32[]{:S(2)}) %all-to-all-start.1) | async-done | bytes 1048608 | tf_op jit(solution)/shard_map/all_to_all | solution.py:150
  113.1 0.3 copy_bitcast_fusion
  113.6 37.2 %all-gather.3.cloned.1.call-done = bf16[256,2048]{0,1:T(8,128)(2,1)} async-done(((bf16[256,64]{0,1:T(8,128)(2,1)}), bf16[256,2048]{0,1:T(8,128)(2,1)}) %all-gather.3.cloned.1.call-update) | async-done | bytes 1048592 | tf_op jit(solution)/shard_map/all_gather | solution.py:92
  150.8 1.6 fusion
  152.5 0.5 convolution_bitcast_fusion
  153.3 0.5 convolution_convert_fusion.2
  153.8 41.5 %all_gather.18 = bf16[256,512]{0,1:T(8,128)(2,1)S(1)} all-gather(bf16[256,16]{0,1:T(8,128)(2,1)S(1)} %convolution_convert_fusion.2), channel_id=1, replica_groups=mesh['dp'=16,'tensor'=32] {'tensor'}, dimensions={1}, use_global_device_ids=true | all-gather | bytes 270336 | tf_op jit(solution)/shard_map/all_gather | solution.py:104
  195.4 0.5 convolution_convert_fusion.3
  195.8 38.9 %all_gather.17 = bf16[256,512]{0,1:T(8,128)(2,1)S(1)} all-gather(bf16[256,16]{0,1:T(8,128)(2,1)S(1)} %convolution_convert_fusion.3), channel_id=1, replica_groups=mesh['dp'=16,'tensor'=32] {'tensor'}, dimensions={1}, use_global_device_ids=true | all-gather | bytes 270336 | tf_op jit(solution)/shard_map/all_gather | solution.py:103
  235.0 0.3 fusion.82
  235.2 0.3 fusion.83
  235.7 0.2 select_reduce_fusion.1
  235.9 0.2 select_reduce_fusion
  237.0 0.2 fusion.10
  237.2 0.2 fusion.12
  237.7 1.5 convolution_convert_fusion.1
  239.2 147.1 %reduce-scatter.3.cloned.1.call-done = bf16[256,64]{0,1:T(8,128)(2,1)} async-done(((bf16[256,2048]{0,1:T(8,128)(2,1)}), bf16[256,64]{0,1:T(8,128)(2,1)}) %reduce-scatter.3.cloned.1.call-update) | async-done | bytes 32784 | tf_op jit(solution)/shard_map/reduce_scatter | solution.py:184
  386.3 1.4 add_convert_fusion
  387.8 59.3 %all-gather.5.cloned.1.call-done = bf16[256,2048]{0,1:T(8,128)(2,1)} async-done(((bf16[256,64]{0,1:T(8,128)(2,1)}), bf16[256,2048]{0,1:T(8,128)(2,1)}) %all-gather.5.cloned.1.call-update) | async-done | bytes 1048592 | tf_op jit(solution)/shard_map/all_gather | solution.py:188
  447.1 1.6 fusion.3
  448.8 2.1 fusion.15
  450.9 4.1 convolution_convert_fusion
  455.1 148.5 %reduce-scatter.5.cloned.1.call-done = bf16[256,64]{0,1:T(8,128)(2,1)} async-done(((bf16[256,2048]{0,1:T(8,128)(2,1)}), bf16[256,64]{0,1:T(8,128)(2,1)}) %reduce-scatter.5.cloned.1.call-update) | async-done | bytes 32784 | tf_op jit(solution)/shard_map/reduce_scatter | solution.py:194
  603.6 0.8 select_convert_fusion
  604.5 0.7 reshape.709
  605.2 10.2 %all-to-all-start.2 = ((bf16[16,2,512]{2,1,0:T(2,128)(2,1)}), bf16[16,2,512]{2,1,0:T(2,128)(2,1)S(1)}, u32[]{:S(2)}, u32[]{:S(2)}) async-start(bf16[16,2,512]{2,1,0:T(2,128)(2,1)} %reshape.709), calls=%async_computation.4 | async-start | bytes 65536 | tf_op jit(solution)/shard_map/all_to_all | solution.py:203
  615.4 0.6 copy_bitcast_fusion.3
  616.0 10.5 %all-to-all-done.2 = bf16[16,2,512]{2,1,0:T(2,128)(2,1)S(1)} async-done(((bf16[16,2,512]{2,1,0:T(2,128)(2,1)}), bf16[16,2,512]{2,1,0:T(2,128)(2,1)S(1)}, u32[]{:S(2)}, u32[]{:S(2)}) %all-to-all-start.2) | async-done | bytes 32800 | tf_op jit(solution)/shard_map/all_to_all | solution.py:203
  626.8 1.5 scatter_fusion
  628.3 0.6 copy-done.9
  (85 shorter events, 3.1 us)
Async XLA Ops:
  7.2 443.7 %copy-start = (bf16[256,2048]{1,0:T(8,128)(2,1)S(1)}, bf16[256,2048]{1,0:T(8,128)(2,1)}, u32[]{:S(2)}) copy-start(bf16[256,2048]{1,0:T(8,128)(2,1)} %param.39) | copy-start | bytes 3145732
  10.9 67.7 %all-to-all-start = ((bf16[16,2,512]{2,1,0:T(2,128)(2,1)}), bf16[16,2,512]{2,1,0:T(2,128)(2,1)S(1)}, u32[]{:S(2)}, u32[]{:S(2)}) async-start(bf16[16,2,512]{2,1,0:T(2,128)(2,1)} %reshape.707), calls=%async_computation | async-start | bytes 65536 | tf_op jit(solution)/shard_map/all_to_all | solution.py:82
  78.6 6.8 %copy-start.1 = (s32[32]{0:T(128)S(1)}, s32[32]{0:T(128)}, u32[]{:S(2)}) copy-start(s32[32]{0:T(128)} %param.29) | copy-start | bytes 388
  78.6 8.4 %copy-start.2 = (s32[32,1]{0,1:T(1,128)S(1)}, s32[32,1]{0,1:T(1,128)}, u32[]{:S(2)}) copy-start(s32[32,1]{0,1:T(1,128)} %param.27) | copy-start | bytes 388
  78.6 34.5 %all-to-all-start.1 = ((bf16[16,8,32,128]{3,1,0,2:T(8,128)(2,1)}), bf16[16,8,32,128]{3,1,0,2:T(8,128)(2,1)S(1)}, u32[]{:S(2)}, u32[]{:S(2)}) async-start(bf16[16,8,32,128]{3,1,0,2:T(8,128)(2,1)} %bitcast.9), calls=%async_computation.1 | async-start | bytes 2097152 | tf_op jit(solution)/shard_map/all_to_all | solution.py:150
  85.3 2.4 copy-start.3
  85.3 3.0 copy-start.4
  85.3 65.6 %all-gather.3.cloned.1.call-start = ((), (), s32[]{:S(2)}) async-start(), calls=%async_computation.5 | async-start | bytes 1081344 | tf_op jit(solution)/shard_map/all_gather | solution.py:92
  86.0 6.1 copy-start.11
  86.9 299.5 %reduce-scatter.3.cloned.1.call-start = ((), (), s32[]{:S(2)}) async-start(), calls=%async_computation.6 | async-start | bytes 1081344 | tf_op jit(solution)/shard_map/reduce_scatter | solution.py:184
  113.4 39.1 %copy-start.13 = (bf16[2048,64]{0,1:T(8,128)(2,1)S(1)}, bf16[2048,64]{0,1:T(8,128)(2,1)}, u32[]{:S(2)}) copy-start(bf16[2048,64]{0,1:T(8,128)(2,1)} %param.32) | copy-start | bytes 786436
  150.8 1.6 copy-start.5
  152.5 0.8 copy-start.14
  153.3 42.0 %copy-start.15 = (bf16[2048,16]{0,1:T(8,128)(2,1)S(1)}, bf16[2048,16]{0,1:T(8,128)(2,1)}, u32[]{:S(2)}) copy-start(bf16[2048,16]{0,1:T(8,128)(2,1)} %param.33) | copy-start | bytes 196612
  235.6 2.1 copy-start.10
  237.7 148.7 %copy-start.7 = (bf16[256,64]{0,1:T(8,128)(2,1)S(1)}, bf16[256,64]{0,1:T(8,128)(2,1)}, u32[]{:S(2)}) copy-start(bf16[256,64]{0,1:T(8,128)(2,1)} %copy.51) | copy-start | bytes 98308
  237.7 150.1 %copy-start.12 = (bf16[2048]{0:T(1024)(128)(2,1)S(1)}, bf16[2048]{0:T(1024)(128)(2,1)}, u32[]{:S(2)}) copy-start(bf16[2048]{0:T(1024)(128)(2,1)} %param.36) | copy-start | bytes 12292
  239.2 207.9 %all-gather.5.cloned.1.call-start = ((), (), s32[]{:S(2)}) async-start(), calls=%async_computation.7 | async-start | bytes 1081344 | tf_op jit(solution)/shard_map/all_gather | solution.py:188
  387.7 215.8 %reduce-scatter.5.cloned.1.call-start = ((), (), s32[]{:S(2)}) async-start(), calls=%async_computation.8 | async-start | bytes 1081344 | tf_op jit(solution)/shard_map/reduce_scatter | solution.py:194
  447.1 1.6 copy-start.6
  454.9 148.7 %copy-start.8 = (bf16[256,64]{0,1:T(8,128)(2,1)S(1)}, bf16[256,64]{0,1:T(8,128)(2,1)}, u32[]{:S(2)}) copy-start(bf16[256,64]{0,1:T(8,128)(2,1)} %add_convert_fusion) | copy-start | bytes 98308
  605.2 21.4 %all-to-all-start.2 = ((bf16[16,2,512]{2,1,0:T(2,128)(2,1)}), bf16[16,2,512]{2,1,0:T(2,128)(2,1)S(1)}, u32[]{:S(2)}, u32[]{:S(2)}) async-start(bf16[16,2,512]{2,1,0:T(2,128)(2,1)} %reshape.709), calls=%async_computation.4 | async-start | bytes 65536 | tf_op jit(solution)/shard_map/all_to_all | solution.py:203
  628.3 0.6 copy-start.9
Sparse Core Ops, SparseCore 0:
  88.8 61.9 all-gather.2
  239.3 146.9 reduce-scatter.2
  389.1 58.0 all-gather.4
  455.1 148.4 reduce-scatter.4
where the time goes:
time: 636 us; the launch traced here: 635 us
  waiting for transfers between devices  420 us (66%)
  blocking collectives  130 us (20%)
  starting transfers between devices  33.1 us (5%)
  between operations  18.1 us (3%)
  local copies, waits for them, and re-layouts  13.2 us (2%)
  matrix products  11 us (2%)
  other arithmetic  10.2 us (2%)
    reduce_scatter x1, waiting for transfers between devices, shards(): lax.psum_scatter(down_terms.astype(jnp.bfloat16), 'tensor', scatter_dimen...  149 us
    reduce_scatter x1, waiting for transfers between devices, shards(): lax.psum_scatter(attn_terms.astype(jnp.bfloat16), 'tensor', scatter_dimen...  147 us
    all_gather x1, waiting for transfers between devices, shards(): middle_rows = lax.all_gather(middle, 'tensor', axis=1, tiled=True)  59.3 us
    all_gather x1, blocking collectives, shards(): all_rows = lax.all_gather(prefix_cache, 'dp', axis=0, tiled=True)  49.1 us
    all_gather x1, blocking collectives, shards(): lax.all_gather(value_part, 'tensor', axis=1, tiled=True)  41.5 us
    all_gather x1, blocking collectives, shards(): lax.all_gather(key_part, 'tensor', axis=1, tiled=True)  38.9 us
    all_gather x1, waiting for transfers between devices, shards(): full_rows = lax.all_gather(state_shard, 'tensor', axis=1, tiled=True)  37.2 us
    all_to_all x1, waiting for transfers between devices, shards(): lax.all_to_all(chosen, 'tensor', split_axis=2, concat_axis=1, tiled=True)  17.5 us
  transfers between devices with their start and end apart: 7, of which 6 were waited for; matrix products, arithmetic and copies ran while one was open for 2% of the time, Pallas kernels for 0%

commit v1 on v0

--- a/solution.py
+++ b/solution.py
@@ -144,7 +144,9 @@
             for request in range(local_reqs)
         )
     )
-    all_rows = lax.all_gather(prefix_cache, "dp", axis=0, tiled=True)
+    all_rows = jnp.concatenate(
+        lax.all_to_all(jnp.stack([prefix_cache] * lax.axis_size("dp")), "dp", 0, 0), axis=0
+    )
     rows_each = all_rows.shape[1]
     chosen = jnp.take(all_rows.reshape(dp_count, rows_each, KVH, 2 * HD), dest_table, axis=2)
     picked = lax.all_to_all(chosen, "tensor", split_axis=2, concat_axis=1, tiled=True).reshape(

time: 636 us -> 601 us (0.945)
  blocking collectives: 130 us -> 80.2 us
  waiting for transfers between devices: 420 us -> 428 us
    all_gather x1 -> x0, blocking collectives: 49.1 us -> none  [shards(): all_rows = lax.all_gather(prefix_cache, 'dp', axis=0, tiled=True)]
    all_to_all x1, waiting for transfers between devices: 17.5 us -> 0.01 us  [shards(): lax.all_to_all(chosen, 'tensor', split_axis=2, concat_axis=1, tiled=True)]
    all_to_all x1, waiting for transfers between devices: 0.01 us -> 11.2 us  [shards(): lax.all_to_all(routed, 'dp', split_axis=0, concat_axis=1, tiled=True)]
    all_gather x1, waiting for transfers between devices: 37.2 us -> 47.9 us  [shards(): full_rows = lax.all_gather(state_shard, 'tensor', axis=1, tiled=True)]
  transfers between devices with their start and end apart: 7 -> 8, of which waited for: 6 -> 7; matrix products, arithmetic and copies ran while one was open for 2% -> 2% of each run, Pallas kernels for 0% -> 0%
where the time goes in v1:
time: 601 us; the launch traced here: 600 us
  waiting for transfers between devices  428 us (71%)
  blocking collectives  80.2 us (13%)
  starting transfers between devices  38.5 us (6%)
  between operations  18.1 us (3%)
  local copies, waits for them, and re-layouts  15.3 us (3%)
  matrix products  11 us (2%)
  other arithmetic  9.54 us (2%)
    reduce_scatter x1, waiting for transfers between devices, shards(): lax.psum_scatter(down_terms.astype(jnp.bfloat16), 'tensor', scatter_dimen...  149 us
    reduce_scatter x1, waiting for transfers between devices, shards(): lax.psum_scatter(attn_terms.astype(jnp.bfloat16), 'tensor', scatter_dimen...  147 us
    all_gather x1, waiting for transfers between devices, shards(): middle_rows = lax.all_gather(middle, 'tensor', axis=1, tiled=True)  59.7 us
    all_gather x1, waiting for transfers between devices, shards(): full_rows = lax.all_gather(state_shard, 'tensor', axis=1, tiled=True)  47.9 us
    all_gather x1, blocking collectives, shards(): lax.all_gather(value_part, 'tensor', axis=1, tiled=True)  41.2 us
    all_gather x1, blocking collectives, shards(): lax.all_gather(key_part, 'tensor', axis=1, tiled=True)  38.9 us
    all_to_all x1, starting transfers between devices, shards(): lax.all_to_all(routed, 'dp', split_axis=0, concat_axis=1, tiled=True)  16 us
  transfers between devices with their start and end apart: 8, of which 7 were waited for; matrix products, arithmetic and copies ran while one was open for 2% of the time, Pallas kernels for 0%

profile of v1, /device:TPU:8, one launch (start us, length us, event | category | flops | bytes accessed | tf_op | source)
XLA Modules:
  0.0 600.2 jit_solution(7727691670454854566)
XLA Ops:
  7.2 0.8 compare_select_fusion.3
  7.9 0.7 compare_and_fusion.1
  8.6 1.4 gather_fusion
  10.2 0.7 reshape.706
  10.9 16.0 %all-to-all-start = ((bf16[16,2,512]{2,1,0:T(2,128)(2,1)}), bf16[16,2,512]{2,1,0:T(2,128)(2,1)S(1)}, u32[]{:S(2)}, u32[]{:S(2)}) async-start(bf16[16,2,512]{2,1,0:T(2,128)(2,1)} %reshape.706), calls=%async_computation | async-start | bytes 65536 | tf_op jit(solution)/shard_map/all_to_all | solution.py:82
  26.9 11.2 %all-to-all-done = bf16[16,2,512]{2,1,0:T(2,128)(2,1)S(1)} async-done(((bf16[16,2,512]{2,1,0:T(2,128)(2,1)}), bf16[16,2,512]{2,1,0:T(2,128)(2,1)S(1)}, u32[]{:S(2)}, u32[]{:S(2)}) %all-to-all-start) | async-done | bytes 32800 | tf_op jit(solution)/shard_map/all_to_all | solution.py:82
  38.1 1.5 stack.2
  39.5 4.8 all-to-all-start.1
  44.5 0.7 copy.51
  45.3 0.6 gather_fusion.3
  46.0 0.6 gather_fusion.5
  46.6 0.6 gather_fusion.4
  47.3 0.6 gather_fusion.2
  48.0 0.7 fusion.80
  48.6 0.6 iota_compare_fusion.2
  49.3 0.6 fusion.81
  49.9 0.6 iota_compare_fusion.1
  54.7 2.9 all-to-all-done.1
  57.6 1.9 gather_fusion.1
  59.5 7.4 %all-to-all-start.2 = ((bf16[16,8,32,128]{3,1,0,2:T(8,128)(2,1)}), bf16[16,8,32,128]{3,1,0,2:T(8,128)(2,1)S(1)}, u32[]{:S(2)}, u32[]{:S(2)}) async-start(bf16[16,8,32,128]{3,1,0,2:T(8,128)(2,1)} %bitcast.10), calls=%async_computation.2 | async-start | bytes 2097152 | tf_op jit(solution)/shard_map/all_to_all | solution.py:152
  66.9 47.9 %all-gather.3.cloned.1.call-done = bf16[256,2048]{0,1:T(8,128)(2,1)} async-done(((bf16[256,64]{0,1:T(8,128)(2,1)}), bf16[256,2048]{0,1:T(8,128)(2,1)}) %all-gather.3.cloned.1.call-update) | async-done | bytes 1048592 | tf_op jit(solution)/shard_map/all_gather | solution.py:92
  114.8 1.6 fusion
  116.4 0.5 convolution_convert_fusion.2
  116.9 41.2 %all_gather.14 = bf16[256,512]{0,1:T(8,128)(2,1)S(1)} all-gather(bf16[256,16]{0,1:T(8,128)(2,1)S(1)} %convolution_convert_fusion.2), channel_id=1, replica_groups=mesh['dp'=16,'tensor'=32] {'tensor'}, dimensions={1}, use_global_device_ids=true | all-gather | bytes 270336 | tf_op jit(solution)/shard_map/all_gather | solution.py:104
  158.2 0.5 convolution_convert_fusion.3
  158.6 38.9 %all_gather.13 = bf16[256,512]{0,1:T(8,128)(2,1)S(1)} all-gather(bf16[256,16]{0,1:T(8,128)(2,1)S(1)} %convolution_convert_fusion.3), channel_id=1, replica_groups=mesh['dp'=16,'tensor'=32] {'tensor'}, dimensions={1}, use_global_device_ids=true | all-gather | bytes 270336 | tf_op jit(solution)/shard_map/all_gather | solution.py:103
  197.9 0.7 copy-done.14
  198.6 0.5 convolution_bitcast_fusion
  199.3 0.2 select_reduce_fusion.1
  199.5 0.2 select_reduce_fusion
  199.8 0.3 copy_bitcast_fusion
  200.3 0.3 fusion.82
  200.6 0.3 fusion.83
  202.4 1.5 convolution_convert_fusion.1
  204.0 146.8 %reduce-scatter.3.cloned.1.call-done = bf16[256,64]{0,1:T(8,128)(2,1)} async-done(((bf16[256,2048]{0,1:T(8,128)(2,1)}), bf16[256,64]{0,1:T(8,128)(2,1)}) %reduce-scatter.3.cloned.1.call-update) | async-done | bytes 32784 | tf_op jit(solution)/shard_map/reduce_scatter | solution.py:186
  350.7 1.4 add_convert_fusion
  352.2 59.7 %all-gather.5.cloned.1.call-done = bf16[256,2048]{0,1:T(8,128)(2,1)} async-done(((bf16[256,64]{0,1:T(8,128)(2,1)}), bf16[256,2048]{0,1:T(8,128)(2,1)}) %all-gather.5.cloned.1.call-update) | async-done | bytes 1048592 | tf_op jit(solution)/shard_map/all_gather | solution.py:190
  411.9 1.6 fusion.3
  413.6 2.1 fusion.15
  415.6 4.1 convolution_convert_fusion
  419.8 148.5 %reduce-scatter.5.cloned.1.call-done = bf16[256,64]{0,1:T(8,128)(2,1)} async-done(((bf16[256,2048]{0,1:T(8,128)(2,1)}), bf16[256,64]{0,1:T(8,128)(2,1)}) %reduce-scatter.5.cloned.1.call-update) | async-done | bytes 32784 | tf_op jit(solution)/shard_map/reduce_scatter | solution.py:196
  568.4 0.8 select_convert_fusion
  569.3 0.7 reshape.708
  570.0 10.1 %all-to-all-start.3 = ((bf16[16,2,512]{2,1,0:T(2,128)(2,1)}), bf16[16,2,512]{2,1,0:T(2,128)(2,1)S(1)}, u32[]{:S(2)}, u32[]{:S(2)}) async-start(bf16[16,2,512]{2,1,0:T(2,128)(2,1)} %reshape.708), calls=%async_computation.5 | async-start | bytes 65536 | tf_op jit(solution)/shard_map/all_to_all | solution.py:205
  580.2 0.6 copy_bitcast_fusion.3
  580.8 10.5 %all-to-all-done.3 = bf16[16,2,512]{2,1,0:T(2,128)(2,1)S(1)} async-done(((bf16[16,2,512]{2,1,0:T(2,128)(2,1)}), bf16[16,2,512]{2,1,0:T(2,128)(2,1)S(1)}, u32[]{:S(2)}, u32[]{:S(2)}) %all-to-all-start.3) | async-done | bytes 32800 | tf_op jit(solution)/shard_map/all_to_all | solution.py:205
  591.5 1.5 scatter_fusion
  593.0 0.6 copy-done.9
  (89 shorter events, 3.5 us)
Async XLA Ops:
  7.2 408.5 %copy-start = (bf16[256,2048]{1,0:T(8,128)(2,1)S(1)}, bf16[256,2048]{1,0:T(8,128)(2,1)}, u32[]{:S(2)}) copy-start(bf16[256,2048]{1,0:T(8,128)(2,1)} %param.39) | copy-start | bytes 3145732
  7.2 38.1 %copy-start.1 = (s32[32]{0:T(128)S(1)}, s32[32]{0:T(128)}, u32[]{:S(2)}) copy-start(s32[32]{0:T(128)} %param.29) | copy-start | bytes 388
  8.6 37.4 %copy-start.2 = (s32[32,1]{0,1:T(1,128)S(1)}, s32[32,1]{0,1:T(1,128)}, u32[]{:S(2)}) copy-start(s32[32,1]{0,1:T(1,128)} %param.27) | copy-start | bytes 388
  10.9 27.2 %all-to-all-start = ((bf16[16,2,512]{2,1,0:T(2,128)(2,1)}), bf16[16,2,512]{2,1,0:T(2,128)(2,1)S(1)}, u32[]{:S(2)}, u32[]{:S(2)}) async-start(bf16[16,2,512]{2,1,0:T(2,128)(2,1)} %reshape.706), calls=%async_computation | async-start | bytes 65536 | tf_op jit(solution)/shard_map/all_to_all | solution.py:82
  39.5 7.1 %copy-start.3 = (s32[32]{0:T(128)S(1)}, s32[32]{0:T(128)}, u32[]{:S(2)}) copy-start(s32[32]{0:T(128)} %param.26) | copy-start | bytes 388
  39.5 18.1 %all-to-all-start.1 = ((bf16[16,1,8,1024]{3,2,1,0:T(8,128)(2,1)}), bf16[16,1,8,1024]{3,2,1,0:T(8,128)(2,1)S(1)}, u32[]{:S(2)}, u32[]{:S(2)}) async-start(bf16[16,1,8,1024]{3,2,1,0:T(8,128)(2,1)} %stack.2), calls=%async_computation.1 | async-start | bytes 524288 | tf_op jit(solution)/shard_map/all_to_all | solution.py:148
  44.3 3.0 copy-start.4
  44.3 70.4 %all-gather.3.cloned.1.call-start = ((), (), s32[]{:S(2)}) async-start(), calls=%async_computation.6 | async-start | bytes 1081344 | tf_op jit(solution)/shard_map/all_gather | solution.py:92
  45.3 7.8 %copy-start.11 = (bf16[2048]{0:T(1024)(128)(2,1)S(1)}, bf16[2048]{0:T(1024)(128)(2,1)}, u32[]{:S(2)}) copy-start(bf16[2048]{0:T(1024)(128)(2,1)} %param.31) | copy-start | bytes 12292
  45.3 9.1 %copy-start.13 = (s32[32]{0:T(128)S(1)}, s32[32]{0:T(128)}, u32[]{:S(2)}) copy-start(s32[32]{0:T(128)} %constant.238) | copy-start | bytes 388
  59.5 56.9 %copy-start.15 = (bf16[2048,16]{0,1:T(8,128)(2,1)S(1)}, bf16[2048,16]{0,1:T(8,128)(2,1)}, u32[]{:S(2)}) copy-start(bf16[2048,16]{0,1:T(8,128)(2,1)} %param.34) | copy-start | bytes 196612
  59.5 140.3 %all-to-all-start.2 = ((bf16[16,8,32,128]{3,1,0,2:T(8,128)(2,1)}), bf16[16,8,32,128]{3,1,0,2:T(8,128)(2,1)S(1)}, u32[]{:S(2)}, u32[]{:S(2)}) async-start(bf16[16,8,32,128]{3,1,0,2:T(8,128)(2,1)} %bitcast.10), calls=%async_computation.2 | async-start | bytes 2097152 | tf_op jit(solution)/shard_map/all_to_all | solution.py:152
  66.9 283.9 %reduce-scatter.3.cloned.1.call-start = ((), (), s32[]{:S(2)}) async-start(), calls=%async_computation.7 | async-start | bytes 1081344 | tf_op jit(solution)/shard_map/reduce_scatter | solution.py:186
  114.8 1.6 copy-start.5
  116.4 41.8 %copy-start.16 = (bf16[2048,16]{0,1:T(8,128)(2,1)S(1)}, bf16[2048,16]{0,1:T(8,128)(2,1)}, u32[]{:S(2)}) copy-start(bf16[2048,16]{0,1:T(8,128)(2,1)} %param.33) | copy-start | bytes 196612
  197.6 1.0 copy-start.14
  200.1 2.4 copy-start.10
  202.4 148.3 %copy-start.7 = (bf16[256,64]{0,1:T(8,128)(2,1)S(1)}, bf16[256,64]{0,1:T(8,128)(2,1)}, u32[]{:S(2)}) copy-start(bf16[256,64]{0,1:T(8,128)(2,1)} %copy.51) | copy-start | bytes 98308
  202.4 149.8 %copy-start.12 = (bf16[2048]{0:T(1024)(128)(2,1)S(1)}, bf16[2048]{0:T(1024)(128)(2,1)}, u32[]{:S(2)}) copy-start(bf16[2048]{0:T(1024)(128)(2,1)} %param.36) | copy-start | bytes 12292
  203.9 208.0 %all-gather.5.cloned.1.call-start = ((), (), s32[]{:S(2)}) async-start(), calls=%async_computation.8 | async-start | bytes 1081344 | tf_op jit(solution)/shard_map/all_gather | solution.py:190
  352.1 216.2 %reduce-scatter.5.cloned.1.call-start = ((), (), s32[]{:S(2)}) async-start(), calls=%async_computation.9 | async-start | bytes 1081344 | tf_op jit(solution)/shard_map/reduce_scatter | solution.py:196
  411.9 1.6 copy-start.6
  419.7 148.7 %copy-start.8 = (bf16[256,64]{0,1:T(8,128)(2,1)S(1)}, bf16[256,64]{0,1:T(8,128)(2,1)}, u32[]{:S(2)}) copy-start(bf16[256,64]{0,1:T(8,128)(2,1)} %add_convert_fusion) | copy-start | bytes 98308
  570.0 21.3 %all-to-all-start.3 = ((bf16[16,2,512]{2,1,0:T(2,128)(2,1)}), bf16[16,2,512]{2,1,0:T(2,128)(2,1)S(1)}, u32[]{:S(2)}, u32[]{:S(2)}) async-start(bf16[16,2,512]{2,1,0:T(2,128)(2,1)} %reshape.708), calls=%async_computation.5 | async-start | bytes 65536 | tf_op jit(solution)/shard_map/all_to_all | solution.py:205
  593.0 0.6 copy-start.9
Sparse Core Ops, SparseCore 0:
  47.9 66.8 all-gather.2
  204.1 146.6 reduce-scatter.2
  353.5 58.4 all-gather.4
  419.9 148.4 reduce-scatter.4
